TPU v7x, 256 devices: a whole 4x4x8 slice. The times are simulated.
256 devices in a mesh: seq: 32 (over x, z), row: 2 (over core), col: 4 (over y).
Axes of the slice: x: 4, y: 4, z: 8, core: 2. Of those that a mesh axis runs over, the one named last changes fastest.
Arguments:
- hidden: bfloat16 [16384, 4096], P(('seq', 'row'), 'col'), may hold values from -6 to 6
- w_x: bfloat16 [4096, 4, 1024], P('col', None, 'row'), may hold values from -0.09375 to 0.09375
- w_z: bfloat16 [4096, 4, 1024], P('col', None, 'row'), may hold values from -0.09375 to 0.09375
- w_bc: bfloat16 [4096, 4, 256], P('col'), may hold values from -0.09375 to 0.09375
- w_dt: bfloat16 [4096, 4, 16], P('col', None, 'row'), may hold values from -0.09375 to 0.09375
- conv_x_w: bfloat16 [4, 4, 1024], P(None, 'col', 'row'), may hold values from -3 to 3
- conv_bc_w: bfloat16 [4, 4, 256], P(None, 'col'), may hold values from -3 to 3
- conv_x_bias: bfloat16 [4, 1024], P('col', 'row'), may hold values from -3 to 3
- conv_bc_bias: bfloat16 [4, 256], P('col'), may hold values from -3 to 3
- dt_bias: float32 [4, 16], P('col', 'row'), may hold values from -5 to -2
- decay_rate: float32 [4, 16], P('col', 'row'), may hold values from 0.005 to 2
- d_skip: float32 [4, 16], P('col', 'row'), may hold values from 0.5 to 1.5
- norm_gain: float32 [4, 1024], P('col', 'row'), may hold values from 0.5 to 1.5
- starts: int32 [16384], P('seq'), may hold values from 0 to 1, as said below
- init_states: float32 [96, 4, 16, 64, 128], P('seq', 'col', 'row'), may hold values from -1.2 to 1.2
- conv_x_edges: bfloat16 [96, 3, 4, 1024], P('seq', None, 'col', 'row'), may hold values from -6 to 6
- conv_bc_edges: bfloat16 [96, 3, 4, 256], P('seq', None, 'col'), may hold values from -6 to 6
Outputs:
- gated_out: bfloat16 [16384, 4, 1024], P('seq', 'col', 'row')
- final_states: float32 [96, 4, 16, 64, 128], P('seq', 'col', 'row')
Inputs may be any that keep to these rules, and one draw needn't show every extreme that they name: The first token of all has starts 1. The 512 tokens of one index of seq hold at most 3 ones, and some index holds exactly 3. The last two indices of seq each hold one or more ones. Slot j of an index of seq in init_states, conv_x_edges, conv_bc_edges and final_states belongs to the j-th request that begins among its tokens; the others are not read.
All inputs are finite; a program needn't handle non-finite values.
Results may differ from a plain program's by a relative error of at most 0.0057.
Values may be sent and summed in bfloat16 or wider, within the bound.
No kernel may reach another device: no remote copies, remote signals or barrier semaphores. Data moves between devices by JAX's collectives and lax.ppermute only.
A program may use at most 128 MiB of HBM per device.

v0:
```python
import jax
import jax.numpy as jnp
from jax import lax
from jax.sharding import PartitionSpec as P

P_SIZE = 64
N = 128
PRECISE = lax.Precision.HIGHEST
EPSILON = 1e-05


def from_behind(value, axis, steps):
    count = lax.axis_size(axis)
    first, last = (max(0, -steps), min(count, count - steps))
    return lax.ppermute(value, axis, [(source, source + steps) for source in range(first, last)])


def local_terms(x_vals, b_proj, c_proj, dt_vals, flag_vals, init_vals, rate_vals):
    rows_here = x_vals.shape[0]
    slot_total = init_vals.shape[0]
    positions = jnp.arange(rows_here, dtype=jnp.int32)
    segment = jnp.cumsum(flag_vals.astype(jnp.int32))
    started = segment[rows_here - 1]
    log_decay = -dt_vals * rate_vals[None, :]
    cumulative = jnp.cumsum(log_decay, axis=0)
    preceding = cumulative - log_decay
    start_at = lax.cummax(jnp.where(flag_vals, positions, 0), axis=0)
    baseline = jnp.where((segment > 0)[:, None], preceding[start_at], 0.0)
    joined = (segment[:, None] == segment[None, :]) & (positions[:, None] >= positions[None, :])
    intersection = jnp.dot(c_proj, b_proj.T, preferred_element_type=jnp.float32)
    cumul_t = cumulative.T
    spread = jnp.where(joined[None], cumul_t[:, :, None] - cumul_t[:, None, :], 0.0)
    mixing = (
        jnp.where(joined[None], jnp.exp(spread), 0.0) * intersection[None] * dt_vals.T[:, None, :]
    )
    internal = jnp.einsum("hij,jhp->ihp", mixing, x_vals.astype(jnp.float32), precision=PRECISE)
    from_slot = jnp.einsum(
        "tn,shpn->tshp", c_proj.astype(jnp.float32), init_vals, precision=PRECISE
    )
    slot_ids = jnp.arange(1, slot_total + 1, dtype=jnp.int32)
    chosen = (segment[:, None] == slot_ids[None, :]).astype(jnp.float32)
    restarted = jnp.einsum("ts,tshp->thp", chosen, from_slot, precision=PRECISE)
    y_part = internal + jnp.exp(cumulative - baseline)[:, :, None] * restarted
    carried = jnp.where((segment == 0)[:, None], jnp.exp(cumulative), 0.0)
    indices = jnp.arange(slot_total + 1, dtype=jnp.int32)
    belongs = segment[:, None] == indices[None, :]
    last_at = jnp.max(jnp.where(belongs, positions[:, None], -1), axis=0)
    first_at = jnp.min(jnp.where(belongs, positions[:, None], rows_here), axis=0)
    cumul_end = jnp.where((last_at >= 0)[:, None], cumulative[jnp.maximum(last_at, 0)], 0.0)
    lag_spread = jnp.where(belongs.T[:, :, None], cumul_end[:, None, :] - cumulative[None], 0.0)
    weights = jnp.where(belongs.T[:, :, None], jnp.exp(lag_spread), 0.0) * dt_vals[None]
    weighted = weights[..., None] * x_vals.astype(jnp.float32)[None]
    gathered = jnp.einsum("sthp,tn->shpn", weighted, b_proj.astype(jnp.float32), precision=PRECISE)
    base_slot = preceding[jnp.minimum(first_at, rows_here - 1)]
    factor = jnp.exp(jnp.where((slot_ids <= started)[:, None], cumul_end[1:] - base_slot[1:], 0.0))
    in_use = slot_ids <= started
    seg_rest = gathered[1:] + jnp.where(
        in_use[:, None, None, None], factor[..., None, None] * init_vals, 0.0
    )
    seg_ends = jnp.concatenate([gathered[:1], seg_rest], axis=0)
    decay_all = jnp.where(started == 0, jnp.exp(cumulative[rows_here - 1]), 0.0)
    state_add = jnp.sum(jnp.where((indices == started)[:, None, None, None], seg_ends, 0.0), axis=0)
    return (y_part, carried, seg_ends, decay_all, state_add, cumul_end[0], started)


def tail_rows(raw, edges, start_last, segment_last, lagged):
    rows_here = raw.shape[0]
    source = jnp.arange(rows_here - lagged, rows_here, dtype=jnp.int32)
    inside = source >= start_last
    row_pick = jnp.clip(lagged - start_last + source, 0, lagged - 1)
    from_edge = edges[jnp.maximum(segment_last - 1, 0), row_pick]
    return jnp.where(inside[:, None], raw[rows_here - lagged :], from_edge)


def convolve(raw, prior, edges, kernel, offset_bias, start_at, segment, positions, lagged):
    rows_here = raw.shape[0]
    slot_total = edges.shape[0]
    extended = jnp.concatenate([prior, raw], axis=0)
    table = edges.reshape(slot_total * lagged, edges.shape[-1])
    total = offset_bias[None].astype(jnp.float32) + kernel[lagged][None].astype(
        jnp.float32
    ) * raw.astype(jnp.float32)
    for offset in range(1, lagged + 1):
        source = positions - offset
        inside = source >= start_at
        row_pick = jnp.clip(lagged - start_at + source, 0, lagged - 1)
        which = jnp.maximum(segment - 1, 0) * lagged + row_pick
        picker = (
            which[:, None] == jnp.arange(slot_total * lagged, dtype=jnp.int32)[None, :]
        ).astype(jnp.bfloat16)
        from_edge = jnp.dot(picker, table, preferred_element_type=jnp.float32)
        earlier = extended[lagged - offset : lagged - offset + rows_here].astype(jnp.float32)
        total = total + kernel[lagged - offset][None].astype(jnp.float32) * jnp.where(
            inside[:, None], earlier, from_edge
        )
    return jax.nn.silu(total).astype(jnp.bfloat16)


def shards(
    hidden,
    w_x,
    w_z,
    w_bc,
    w_dt,
    conv_x_w,
    conv_bc_w,
    conv_x_bias,
    conv_bc_bias,
    dt_bias,
    decay_rate,
    d_skip,
    norm_gain,
    starts,
    init_states,
    conv_x_edges,
    conv_bc_edges,
):
    tokens = lax.all_gather(hidden, "row", axis=0, tiled=True)
    rows_here = tokens.shape[0]
    channels = w_x.shape[2]
    heads_here = w_dt.shape[2]
    lagged = conv_x_w.shape[0] - 1
    pieces = [
        jnp.einsum("td,dgc->gtc", tokens, weight, preferred_element_type=jnp.float32)
        for weight in (w_x, w_z, w_bc, w_dt)
    ]
    summed = lax.psum_scatter(
        jnp.concatenate(pieces, axis=2), "col", scatter_dimension=0, tiled=True
    )
    mixed = summed[0].astype(jnp.bfloat16)
    x_raw = mixed[:, :channels]
    z_gate = mixed[:, channels : 2 * channels]
    bc_raw = mixed[:, 2 * channels : 2 * channels + 2 * N]
    dt_raw = mixed[:, 2 * channels + 2 * N :]
    positions = jnp.arange(rows_here, dtype=jnp.int32)
    flag_vals = starts == 1
    segment = jnp.cumsum(starts)
    start_at = lax.cummax(jnp.where(flag_vals, positions, -lagged), axis=0)
    x_edges = conv_x_edges[:, :, 0]
    bc_edges = conv_bc_edges[:, :, 0]
    start_last = start_at[rows_here - 1]
    segment_last = segment[rows_here - 1]
    send_x = tail_rows(x_raw, x_edges, start_last, segment_last, lagged)
    send_bc = tail_rows(bc_raw, bc_edges, start_last, segment_last, lagged)
    prior_x, prior_bc = from_behind((send_x, send_bc), "seq", 1)
    x_conv = convolve(
        x_raw,
        prior_x,
        x_edges,
        conv_x_w[:, 0],
        conv_x_bias[0],
        start_at,
        segment,
        positions,
        lagged,
    )
    bc_conv = convolve(
        bc_raw,
        prior_bc,
        bc_edges,
        conv_bc_w[:, 0],
        conv_bc_bias[0],
        start_at,
        segment,
        positions,
        lagged,
    )
    x_heads = x_conv.reshape(rows_here, heads_here, P_SIZE)
    b_proj = bc_conv[:, :N]
    c_proj = bc_conv[:, N:]
    dt_vals = jax.nn.softplus(dt_raw.astype(jnp.float32) + dt_bias[0][None, :])
    init_vals = init_states[:, 0]
    y_part, carried, seg_ends, decay_all, state_add, end_zero, started = local_terms(
        x_heads, b_proj, c_proj, dt_vals, flag_vals, init_vals, decay_rate[0]
    )
    seq_count = lax.axis_size("seq")
    seq_at = lax.axis_index("seq")
    heads_n, p_n, n_n = state_add.shape
    ones = jnp.ones((heads_n,), jnp.float32)
    zeros_state = jnp.zeros_like(state_add)
    has_start = jnp.where(started > 0, 1.0, 0.0).astype(jnp.float32)

    def pack(decay, state, mark):
        aux = jnp.concatenate(
            [
                jnp.broadcast_to(decay[:, None], (heads_n, n_n // 2)),
                jnp.broadcast_to(mark, (heads_n, n_n - n_n // 2)),
            ],
            axis=1,
        )
        return jnp.concatenate([state, aux[:, None, :]], axis=1)

    def unpack(packed):
        return (packed[:, p_n, 0], packed[:, :p_n], packed[0, p_n, n_n - 1])

    fwd_in = (decay_all * ones, state_add)
    fwd_ex = (ones, zeros_state)
    bwd_in = (jnp.exp(end_zero), seg_ends[0], has_start)
    bwd_ex = (ones, zeros_state, jnp.zeros((), jnp.float32))
    shift = 1
    while shift < seq_count:
        last = 2 * shift >= seq_count
        got_f = from_behind(pack(fwd_in[0], fwd_in[1], 0.0), "seq", shift)
        got_b = from_behind(pack(*bwd_in), "seq", -shift)
        early_a, early_b, _ = unpack(got_f)
        late_a, late_b, late_m = unpack(got_b)
        late_ok = seq_at + shift < seq_count
        fwd_ex = (fwd_ex[0] * early_a, fwd_ex[0][:, None, None] * early_b + fwd_ex[1])

        def near_far(near, far_a, far_b, far_m):
            keep = (near[2] > 0.5) | jnp.logical_not(late_ok)
            return (
                jnp.where(keep, near[0], far_a * near[0]),
                jnp.where(keep, near[1], far_a[:, None, None] * near[1] + far_b),
                jnp.where(keep, near[2], far_m),
            )

        bwd_ex = near_far(bwd_ex, late_a, late_b, late_m)
        if not last:
            fwd_in = (fwd_in[0] * early_a, fwd_in[0][:, None, None] * early_b + fwd_in[1])
            bwd_in = near_far(bwd_in, late_a, late_b, late_m)
        shift *= 2
    state_in = fwd_ex[1]
    carried_in = jnp.einsum("tn,hpn->thp", c_proj.astype(jnp.float32), state_in, precision=PRECISE)
    y_full = (
        y_part
        + carried[:, :, None] * carried_in
        + d_skip[0][None, :, None] * x_heads.astype(jnp.float32)
    )
    tail_state = bwd_ex[0][:, None, None] * state_add + bwd_ex[1]
    slot_ids = jnp.arange(1, init_vals.shape[0] + 1, dtype=jnp.int32)
    finals = jnp.where(
        (slot_ids < started)[:, None, None, None],
        seg_ends[1:],
        jnp.where((slot_ids == started)[:, None, None, None], tail_state[None], 0.0),
    )
    gated = y_full.reshape(rows_here, channels) * jax.nn.silu(z_gate.astype(jnp.float32))
    partial_sq = jnp.sum(gated * gated, axis=-1)
    total_sq = lax.psum(partial_sq, "row")
    mean_sq = total_sq / (channels * lax.axis_size("row"))
    gated_out = (gated * lax.rsqrt(mean_sq + EPSILON)[:, None] * norm_gain[0][None, :]).astype(
        jnp.bfloat16
    )
    return (gated_out.reshape(rows_here, 1, channels), finals[:, None])


def solution(mesh):
    placed = (
        P(("seq", "row"), "col"),
        P("col", None, "row"),
        P("col", None, "row"),
        P("col", None, None),
        P("col", None, "row"),
        P(None, "col", "row"),
        P(None, "col", None),
        P("col", "row"),
        P("col", None),
        P("col", "row"),
        P("col", "row"),
        P("col", "row"),
        P("col", "row"),
        P("seq"),
        P("seq", "col", "row", None, None),
        P("seq", None, "col", "row"),
        P("seq", None, "col", None),
    )
    return jax.shard_map(
        shards,
        mesh=mesh,
        in_specs=placed,
        out_specs=(P("seq", "col", "row"), P("seq", "col", "row", None, None)),
        check_vma=False,
    )
```

profile of v0, /device:TPU:101, one launch (start us, length us, event | category | flops | bytes accessed | tf_op | source)
XLA Modules:
  0.0 338.3 jit_solution(753345638524201628)
XLA Ops:
  8.0 18.5 %all-gather.2.cloned.1.call-done = bf16[512,1024]{1,0:T(8,128)(2,1)} async-done(((bf16[256,1024]{1,0:T(8,128)(2,1)}), bf16[512,1024]{1,0:T(8,128)(2,1)}) %all-gather.2.cloned.1.call-update) | async-done | bytes 1048592 | tf_op jit(solution)/shard_map/all_gather | solution.py:118
  26.5 1.6 convolution_bitcast_fusion
  28.1 3.3 fusion.30
  31.6 2.7 fusion.23
  34.3 2.7 fusion.20
  37.0 4.4 %pad_maximum_fusion = f32[4,512,1288]{1,2,0:T(8,128)} fusion(f32[4,512,8]{1,2,0:T(8,128)S(1)} %convolution_bitcast_fusion, f32[4,512,256]{1,2,0:T(8,128)S(1)} %fusion.30, f32[4,512,512]{1,2,0:T(8,128)S(1)} %fusion.23, f32[4,512,512]{1,2,0:T(8,128)S(1)} %fusion.20), kind=kLoop, calls=%fused_computation.5 | loop fusion | flops 7913472 | bytes 21102592 | tf_op jit(solution)/shard_map/concatenate | solution.py:128
  54.0 1.2 add_compare_fusion
  55.2 1.2 broadcast_compare_fusion.5
  56.4 1.2 iota_compare_fusion.16
  57.6 1.3 broadcast_compare_fusion.3
  68.7 74.4 %reduce-scatter.2.cloned.1.call-done = f32[1,512,1288]{1,2,0:T(8,128)} async-done(((f32[4,512,1288]{1,2,0:T(8,128)}), f32[1,512,1288]{1,2,0:T(8,128)}) %reduce-scatter.2.cloned.1.call-update) | async-done | bytes 2637840 | tf_op jit(solution)/shard_map/reduce_scatter | solution.py:127
  143.1 1.9 convert_bitcast_fusion
  145.0 1.7 slice_select_fusion
  146.6 4.4 %collective-permute-start = (bf16[3,512]{0,1:T(8,128)(2,1)}, bf16[3,512]{0,1:T(8,128)(2,1)}, u32[]{:S(2)}, u32[]{:S(2)}) collective-permute-start(bf16[3,512]{0,1:T(8,128)(2,1)} %slice_select_fusion), channel_id=1, source_target_pairs={{0,8},{8,16},{16,24},{24,32},{32,40},{40,48},{48,56},{56,64},{64,7... | collective-permute-start | bytes 9224 | tf_op jit(solution)/shard_map/ppermute | solution.py:15
  151.7 2.5 collective-permute-start.1
  154.2 1.4 compare_select_fusion
  156.9 1.3 exponential_select_fusion
  159.0 1.6 gather_fusion.3
  162.3 2.0 multiply_convert_fusion.2
  164.3 2.5 multiply_convert_fusion.1
  167.0 2.2 fusion.11
  169.9 3.0 collective-permute-start.7
  174.6 5.7 %collective-permute-done.7 = f32[8,65,128]{2,1,0:T(8,128)S(1)} collective-permute-done((f32[8,65,128]{2,1,0:T(8,128)S(1)}, f32[8,65,128]{2,1,0:T(8,128)S(1)}, u32[]{:S(2)}, u32[]{:S(2)}) %collective-permute-start.7) | collective-permute-done | bytes 266272 | tf_op jit(solution)/shard_map/ppermute | solution.py:15
  183.1 1.9 collective-permute-start.8
  187.5 1.3 subtract_exponential_fusion
  188.8 12.3 %collective-permute-done.8 = f32[8,65,128]{2,1,0:T(8,128)} collective-permute-done((f32[8,65,128]{2,1,0:T(8,128)}, f32[8,65,128]{2,1,0:T(8,128)}, u32[]{:S(2)}, u32[]{:S(2)}) %collective-permute-start.8) | collective-permute-done | bytes 266272 | tf_op jit(solution)/shard_map/ppermute | solution.py:15
  202.7 1.3 slice.312
  206.6 4.4 %collective-permute-start.9 = (f32[8,65,128]{2,1,0:T(8,128)}, f32[8,65,128]{2,1,0:T(8,128)}, u32[]{:S(2)}, u32[]{:S(2)}) collective-permute-start(f32[8,65,128]{2,1,0:T(8,128)} %pad_maximum_fusion.9), channel_id=1, source_target_pairs={{32,0},{40,8},{48,16},{56,24},{64,32},{72,40},{80,48},{88,56},{96,... | collective-permute-start | bytes 798728 | tf_op jit(solution)/shard_map/ppermute | solution.py:15
  211.0 1.4 slice_add_fusion
  212.4 15.0 %collective-permute-done.9 = f32[8,65,128]{2,1,0:T(8,128)} collective-permute-done((f32[8,65,128]{2,1,0:T(8,128)}, f32[8,65,128]{2,1,0:T(8,128)}, u32[]{:S(2)}, u32[]{:S(2)}) %collective-permute-start.9) | collective-permute-done | bytes 266272 | tf_op jit(solution)/shard_map/ppermute | solution.py:15
  229.0 1.3 slice.315
  232.7 1.9 collective-permute-start.10
  236.5 1.9 collective-permute-start.2
  238.4 4.0 %collective-permute-done.10 = f32[8,65,128]{2,1,0:T(8,128)} collective-permute-done((f32[8,65,128]{2,1,0:T(8,128)}, f32[8,65,128]{2,1,0:T(8,128)}, u32[]{:S(2)}, u32[]{:S(2)}) %collective-permute-start.10) | collective-permute-done | bytes 266272 | tf_op jit(solution)/shard_map/ppermute | solution.py:15
  243.3 1.3 slice.318
  247.0 2.0 collective-permute-start.11
  254.7 1.6 fusion.60
  256.4 2.1 collective-permute-start.3
  258.5 2.3 fusion.51
  260.8 13.4 %collective-permute-done.3 = f32[8,65,128]{2,1,0:T(8,128)S(1)} collective-permute-done((f32[8,65,128]{2,1,0:T(8,128)S(1)}, f32[8,65,128]{2,1,0:T(8,128)S(1)}, u32[]{:S(2)}, u32[]{:S(2)}) %collective-permute-start.3) | collective-permute-done | bytes 266272 | tf_op jit(solution)/shard_map/ppermute | solution.py:15
  275.4 3.2 collective-permute-start.4
  279.4 12.3 %collective-permute-done.4 = f32[8,65,128]{2,1,0:T(8,128)S(1)} collective-permute-done((f32[8,65,128]{2,1,0:T(8,128)S(1)}, f32[8,65,128]{2,1,0:T(8,128)S(1)}, u32[]{:S(2)}, u32[]{:S(2)}) %collective-permute-start.4) | collective-permute-done | bytes 266272 | tf_op jit(solution)/shard_map/ppermute | solution.py:15
  292.1 13.5 %collective-permute-start.5 = (f32[8,65,128]{2,1,0:T(8,128)S(1)}, f32[8,65,128]{2,1,0:T(8,128)S(1)}, u32[]{:S(2)}, u32[]{:S(2)}) collective-permute-start(f32[8,65,128]{2,1,0:T(8,128)S(1)} %pad_maximum_fusion.5), channel_id=1, source_target_pairs={{0,64},{8,72},{16,80},{24,88},{32,96},{40,104},{48,112},{56,120},{... | collective-permute-start | bytes 798728 | tf_op jit(solution)/shard_map/ppermute | solution.py:15
  305.8 6.9 %fusion.38 = f32[512,8,64]{0,2,1:T(8,128)S(1)} fusion(bf16[512,8,64]{0,2,1:T(8,128)(2,1)S(1)} %bitcast.150, f32[8,512]{1,0:T(8,128)S(1)} %copy-done.18, f32[512,512]{1,0:T(8,128)S(1)} %fusion.93, f32[8,512]{1,0:T(8,128)S(1)} %copy-done.20, pred[512,512]{1,0:T(8,128)(4,1)S(1)} %copy-done.8, f32[512,8,64]{0,2,1:T(8,128)S(1)} %bitcast.152, ...), kind=kOutput, calls=%fused_computation.38 | convolution fusion | flops 1621622784 | bytes 3981312 | tf_op jit(solution)/shard_map/hij,jhp->ihp/dot_general | solution.py:36
  313.0 1.3 collective-permute-start.6
  315.4 8.0 %collective-permute-done.6 = f32[8,65,128]{2,1,0:T(8,128)S(1)} collective-permute-done((f32[8,65,128]{2,1,0:T(8,128)S(1)}, f32[8,65,128]{2,1,0:T(8,128)S(1)}, u32[]{:S(2)}, u32[]{:S(2)}) %collective-permute-start.6) | collective-permute-done | bytes 266272 | tf_op jit(solution)/shard_map/ppermute | solution.py:15
  323.4 1.7 fusion.37
  325.5 4.6 %psum.7 = f32[512]{0:T(512)S(1)} all-reduce(f32[512]{0:T(512)S(1)} %multiply_reduce_fusion), channel_id=1, replica_groups=mesh['seq'=32,'row'=2,'col'=4] {'row'}, use_global_device_ids=true, to_apply=%region_15.16 | all-reduce | flops 512 | bytes 4096 | tf_op jit(solution)/shard_map/psum | solution.py:239
  (240 shorter events, 52.4 us)
Async XLA Ops:
  7.2 19.3 %copy-start = (bf16[1024,4,8]{0,2,1:T(8,128)(2,1)S(1)}, bf16[1024,4,8]{0,2,1:T(8,128)(2,1)}, u32[]{:S(2)}) copy-start(bf16[1024,4,8]{0,2,1:T(8,128)(2,1)} %param.21) | copy-start | bytes 196612
  7.2 19.3 %all-gather.2.cloned.1.call-start = ((), (), s32[]{:S(2)}) async-start(), calls=%async_computation.1 | async-start | bytes 1572864 | tf_op jit(solution)/shard_map/all_gather | solution.py:118
  7.9 135.1 %reduce-scatter.2.cloned.1.call-start = ((), (), s32[]{:S(2)}) async-start(), calls=%async_computation.2 | async-start | bytes 13189120 | tf_op jit(solution)/shard_map/reduce_scatter | solution.py:127
  41.4 9.4 %copy-start.32 = (bf16[1,512]{1,0:T(2,128)(2,1)S(1)}, bf16[1,512]{1,0:T(2,128)(2,1)}, u32[]{:S(2)}) copy-start(bf16[1,512]{1,0:T(2,128)(2,1)} %param.24) | copy-start | bytes 3076
  41.4 10.0 %copy-start.11 = (bf16[3,3,1,256]{3,1,2,0:T(4,128)(2,1)S(1)}, bf16[3,3,1,256]{3,1,2,0:T(4,128)(2,1)}, u32[]{:S(2)}) copy-start(bf16[3,3,1,256]{3,1,2,0:T(4,128)(2,1)} %param.33) | copy-start | bytes 13828
  41.4 10.7 %copy-start.37 = (bf16[1,256]{1,0:T(2,128)(2,1)S(1)}, bf16[1,256]{1,0:T(2,128)(2,1)}, u32[]{:S(2)}) copy-start(bf16[1,256]{1,0:T(2,128)(2,1)} %param.25) | copy-start | bytes 1540
  41.4 21.9 %copy-start.24 = (bf16[4,1,256]{2,0,1:T(4,128)(2,1)S(1)}, bf16[4,1,256]{2,0,1:T(4,128)(2,1)}, u32[]{:S(2)}) copy-start(bf16[4,1,256]{2,0,1:T(4,128)(2,1)} %param.23) | copy-start | bytes 6148
  41.5 22.6 %copy-start.21 = (bf16[4,1,512]{2,0,1:T(4,128)(2,1)S(1)}, bf16[4,1,512]{2,0,1:T(4,128)(2,1)}, u32[]{:S(2)}) copy-start(bf16[4,1,512]{2,0,1:T(4,128)(2,1)} %param.22) | copy-start | bytes 12292
  45.3 23.4 %copy-start.10 = (bf16[9,512]{1,0:T(8,128)(2,1)}, bf16[9,512]{1,0:T(8,128)(2,1)S(1)}, u32[]{:S(2)}) copy-start(bf16[9,512]{1,0:T(8,128)(2,1)S(1)} %reshape_squeeze.6) | copy-start | bytes 27652
  143.1 8.0 %copy-start.30 = (pred[3]{0:T(512)(128)(4,1)S(1)}, pred[3]{0:T(512)(128)(4,1)}, u32[]{:S(2)}) copy-start(pred[3]{0:T(512)(128)(4,1)} %add_compare_fusion) | copy-start | bytes 13
  146.6 17.6 %collective-permute-start = (bf16[3,512]{0,1:T(8,128)(2,1)}, bf16[3,512]{0,1:T(8,128)(2,1)}, u32[]{:S(2)}, u32[]{:S(2)}) collective-permute-start(bf16[3,512]{0,1:T(8,128)(2,1)} %slice_select_fusion), channel_id=1, source_target_pairs={{0,8},{8,16},{16,24},{24,32},{32,40},{40,48},{48,56},{56,64},{64,7... | collective-permute-start | bytes 9224 | tf_op jit(solution)/shard_map/ppermute | solution.py:15
  151.7 10.5 %collective-permute-start.1 = (bf16[3,256]{0,1:T(8,128)(2,1)}, bf16[3,256]{0,1:T(8,128)(2,1)}, u32[]{:S(2)}, u32[]{:S(2)}) collective-permute-start(bf16[3,256]{0,1:T(8,128)(2,1)} %slice_select_fusion.1), channel_id=1, source_target_pairs={{0,8},{8,16},{16,24},{24,32},{32,40},{40,48},{48,56},{56,64},{64,7... | collective-permute-start | bytes 4616 | tf_op jit(solution)/shard_map/ppermute | solution.py:15
  164.3 8.7 %copy-start.4 = (bf16[512,256]{0,1:T(8,128)(2,1)}, bf16[512,256]{0,1:T(8,128)(2,1)S(1)}, u32[]{:S(2)}) copy-start(bf16[512,256]{0,1:T(8,128)(2,1)S(1)} %multiply_convert_fusion.2) | copy-start | bytes 786436
  166.8 6.1 %copy-start.2 = (bf16[512,512]{0,1:T(8,128)(2,1)}, bf16[512,512]{0,1:T(8,128)(2,1)S(1)}, u32[]{:S(2)}) copy-start(bf16[512,512]{0,1:T(8,128)(2,1)S(1)} %multiply_convert_fusion.1) | copy-start | bytes 1572868
  166.8 6.1 %copy-start.28 = (f32[1,8]{1,0:T(1,128)S(1)}, f32[1,8]{1,0:T(1,128)}, u32[]{:S(2)}) copy-start(f32[1,8]{1,0:T(1,128)} %param.26) | copy-start | bytes 100
  166.8 18.2 %copy-start.31 = (pred[3]{0:T(512)(128)(4,1)S(1)}, pred[3]{0:T(512)(128)(4,1)}, u32[]{:S(2)}) copy-start(pred[3]{0:T(512)(128)(4,1)} %broadcast_compare_fusion.5) | copy-start | bytes 13
  166.8 18.8 %copy-start.22 = (s32[1024]{0:T(1024)S(1)}, s32[1024]{0:T(1024)}, u32[]{:S(2)}) copy-start(s32[1024]{0:T(1024)} %pad_clamp_fusion.2) | copy-start | bytes 12292
  166.8 13.6 %copy-start.15 = (f32[4,8]{1,0:T(4,128)S(1)}, f32[4,8]{1,0:T(4,128)}, u32[]{:S(2)}) copy-start(f32[4,8]{1,0:T(4,128)} %copy-done.14) | copy-start | bytes 388
  169.9 10.4 %collective-permute-start.7 = (f32[8,65,128]{2,1,0:T(8,128)S(1)}, f32[8,65,128]{2,1,0:T(8,128)S(1)}, u32[]{:S(2)}, u32[]{:S(2)}) collective-permute-start(f32[8,65,128]{2,1,0:T(8,128)S(1)} %pad_maximum_fusion.7), channel_id=1, source_target_pairs={{8,0},{16,8},{24,16},{32,24},{40,32},{48,40},{56,48},{64,56},{72,6... | collective-permute-start | bytes 798728 | tf_op jit(solution)/shard_map/ppermute | solution.py:15
  180.3 24.5 %copy-start.7 = (f32[8,65,128]{2,1,0:T(8,128)}, f32[8,65,128]{2,1,0:T(8,128)S(1)}, u32[]{:S(2)}) copy-start(f32[8,65,128]{2,1,0:T(8,128)S(1)} %collective-permute-done.7) | copy-start | bytes 798724
  183.1 18.0 %collective-permute-start.8 = (f32[8,65,128]{2,1,0:T(8,128)}, f32[8,65,128]{2,1,0:T(8,128)}, u32[]{:S(2)}, u32[]{:S(2)}) collective-permute-start(f32[8,65,128]{2,1,0:T(8,128)} %pad_maximum_fusion.8), channel_id=1, source_target_pairs={{16,0},{24,8},{32,16},{40,24},{48,32},{56,40},{64,48},{72,56},{80,... | collective-permute-start | bytes 798728 | tf_op jit(solution)/shard_map/ppermute | solution.py:15
  188.8 60.3 %copy-start.17 = (f32[8,4]{0,1:T(4,128)S(1)}, f32[8,4]{0,1:T(4,128)}, u32[]{:S(2)}) copy-start(f32[8,4]{0,1:T(4,128)} %copy-done.16) | copy-start | bytes 388
  204.8 29.8 %copy-start.40 = (pred[4]{0:T(512)(128)(4,1)S(1)}, pred[4]{0:T(512)(128)(4,1)}, u32[]{:S(2)}) copy-start(pred[4]{0:T(512)(128)(4,1)} %iota_compare_fusion.16) | copy-start | bytes 16
  204.8 46.9 %copy-start.27 = (f32[8]{0:T(128)S(1)}, f32[8]{0:T(128)}, u32[]{:S(2)}) copy-start(f32[8]{0:T(128)} %get-tuple-element.21) | copy-start | bytes 100
  204.8 49.9 %copy-start.34 = (f32[8]{0:T(128)S(1)}, f32[8]{0:T(128)}, u32[]{:S(2)}) copy-start(f32[8]{0:T(128)} %get-tuple-element.54) | copy-start | bytes 100
  206.6 20.8 %collective-permute-start.9 = (f32[8,65,128]{2,1,0:T(8,128)}, f32[8,65,128]{2,1,0:T(8,128)}, u32[]{:S(2)}, u32[]{:S(2)}) collective-permute-start(f32[8,65,128]{2,1,0:T(8,128)} %pad_maximum_fusion.9), channel_id=1, source_target_pairs={{32,0},{40,8},{48,16},{56,24},{64,32},{72,40},{80,48},{88,56},{96,... | collective-permute-start | bytes 798728 | tf_op jit(solution)/shard_map/ppermute | solution.py:15
  212.4 46.1 %copy-start.1 = (f32[3,1,8,64,128]{4,3,2,1,0:T(8,128)S(1)}, f32[3,1,8,64,128]{4,3,2,1,0:T(8,128)}, u32[]{:S(2)}) copy-start(f32[3,1,8,64,128]{4,3,2,1,0:T(8,128)} %param.31) | copy-start | bytes 2359300
  232.7 9.7 %collective-permute-start.10 = (f32[8,65,128]{2,1,0:T(8,128)}, f32[8,65,128]{2,1,0:T(8,128)}, u32[]{:S(2)}, u32[]{:S(2)}) collective-permute-start(f32[8,65,128]{2,1,0:T(8,128)} %pad_maximum_fusion.10), channel_id=1, source_target_pairs={{64,0},{72,8},{80,16},{88,24},{96,32},{104,40},{112,48},{120,56},{... | collective-permute-start | bytes 798728 | tf_op jit(solution)/shard_map/ppermute | solution.py:15
  236.5 13.8 %collective-permute-start.2 = (f32[8,65,128]{2,1,0:T(8,128)}, f32[8,65,128]{2,1,0:T(8,128)}, u32[]{:S(2)}, u32[]{:S(2)}) collective-permute-start(f32[8,65,128]{2,1,0:T(8,128)} %pad_maximum_fusion.2), channel_id=1, source_target_pairs={{0,8},{8,16},{16,24},{24,32},{32,40},{40,48},{48,56},{56,64},{64,7... | collective-permute-start | bytes 798728 | tf_op jit(solution)/shard_map/ppermute | solution.py:15
  247.0 6.6 %collective-permute-start.11 = (f32[8,65,128]{2,1,0:T(8,128)}, f32[8,65,128]{2,1,0:T(8,128)}, u32[]{:S(2)}, u32[]{:S(2)}) collective-permute-start(f32[8,65,128]{2,1,0:T(8,128)} %pad_maximum_fusion.11), channel_id=1, source_target_pairs={{128,0},{136,8},{144,16},{152,24},{160,32},{168,40},{176,48},{184,... | collective-permute-start | bytes 798728 | tf_op jit(solution)/shard_map/ppermute | solution.py:15
  254.7 20.5 %copy-start.42 = (f32[8]{0:T(128)S(1)}, f32[8]{0:T(128)}, u32[]{:S(2)}) copy-start(f32[8]{0:T(128)} %copy-done.41) | copy-start | bytes 100
  254.7 23.9 %copy-start.13 = (f32[512,3]{0,1:T(4,128)S(1)}, f32[512,3]{0,1:T(4,128)}, u32[]{:S(2)}) copy-start(f32[512,3]{0,1:T(4,128)} %copy.86) | copy-start | bytes 18436
  256.4 22.7 %copy-start.5 = (bf16[512,256]{0,1:T(8,128)(2,1)S(1)}, bf16[512,256]{0,1:T(8,128)(2,1)}, u32[]{:S(2)}) copy-start(bf16[512,256]{0,1:T(8,128)(2,1)} %copy-done.4) | copy-start | bytes 786436
  256.4 17.8 %collective-permute-start.3 = (f32[8,65,128]{2,1,0:T(8,128)S(1)}, f32[8,65,128]{2,1,0:T(8,128)S(1)}, u32[]{:S(2)}, u32[]{:S(2)}) collective-permute-start(f32[8,65,128]{2,1,0:T(8,128)S(1)} %pad_maximum_fusion.3), channel_id=1, source_target_pairs={{0,16},{8,24},{16,32},{24,40},{32,48},{40,56},{48,64},{56,72},{64,... | collective-permute-start | bytes 798728 | tf_op jit(solution)/shard_map/ppermute | solution.py:15
  260.8 44.9 %copy-start.3 = (bf16[512,512]{0,1:T(8,128)(2,1)S(1)}, bf16[512,512]{0,1:T(8,128)(2,1)}, u32[]{:S(2)}) copy-start(bf16[512,512]{0,1:T(8,128)(2,1)} %copy-done.2) | copy-start | bytes 1572868
  260.8 44.9 %copy-start.8 = (pred[512,512]{1,0:T(8,128)(4,1)S(1)}, pred[512,512]{1,0:T(8,128)(4,1)}, u32[]{:S(2)}) copy-start(pred[512,512]{1,0:T(8,128)(4,1)} %fusion.50) | copy-start | bytes 786436
  260.8 44.9 %copy-start.18 = (f32[8,512]{1,0:T(8,128)S(1)}, f32[8,512]{1,0:T(8,128)}, u32[]{:S(2)}) copy-start(f32[8,512]{1,0:T(8,128)} %get-tuple-element.34) | copy-start | bytes 49156
  260.8 44.9 %copy-start.19 = (f32[512,8]{0,1:T(8,128)S(1)}, f32[512,8]{0,1:T(8,128)}, u32[]{:S(2)}) copy-start(f32[512,8]{0,1:T(8,128)} %subtract_exponential_fusion) | copy-start | bytes 49156
  260.8 44.9 %copy-start.20 = (f32[8,512]{1,0:T(8,128)S(1)}, f32[8,512]{1,0:T(8,128)}, u32[]{:S(2)}) copy-start(f32[8,512]{1,0:T(8,128)} %add_bitcast_fusion.1) | copy-start | bytes 49156
  275.4 16.4 %collective-permute-start.4 = (f32[8,65,128]{2,1,0:T(8,128)S(1)}, f32[8,65,128]{2,1,0:T(8,128)S(1)}, u32[]{:S(2)}, u32[]{:S(2)}) collective-permute-start(f32[8,65,128]{2,1,0:T(8,128)S(1)} %pad_maximum_fusion.4), channel_id=1, source_target_pairs={{0,32},{8,40},{16,48},{24,56},{32,64},{40,72},{48,80},{56,88},{64,... | collective-permute-start | bytes 798728 | tf_op jit(solution)/shard_map/ppermute | solution.py:15
  292.1 20.5 %collective-permute-start.5 = (f32[8,65,128]{2,1,0:T(8,128)S(1)}, f32[8,65,128]{2,1,0:T(8,128)S(1)}, u32[]{:S(2)}, u32[]{:S(2)}) collective-permute-start(f32[8,65,128]{2,1,0:T(8,128)S(1)} %pad_maximum_fusion.5), channel_id=1, source_target_pairs={{0,64},{8,72},{16,80},{24,88},{32,96},{40,104},{48,112},{56,120},{... | collective-permute-start | bytes 798728 | tf_op jit(solution)/shard_map/ppermute | solution.py:15
  305.7 8.6 %copy-start.38 = (pred[3]{0:T(512)(128)(4,1)S(1)}, pred[3]{0:T(512)(128)(4,1)}, u32[]{:S(2)}) copy-start(pred[3]{0:T(512)(128)(4,1)} %get-tuple-element.58) | copy-start | bytes 13
  305.7 8.6 %copy-start.39 = (pred[3]{0:T(512)(128)(4,1)S(1)}, pred[3]{0:T(512)(128)(4,1)}, u32[]{:S(2)}) copy-start(pred[3]{0:T(512)(128)(4,1)} %get-tuple-element.59) | copy-start | bytes 13
  305.7 17.7 %copy-start.12 = (f32[512,8]{0,1:T(8,128)S(1)}, f32[512,8]{0,1:T(8,128)}, u32[]{:S(2)}) copy-start(f32[512,8]{0,1:T(8,128)} %get-tuple-element.23) | copy-start | bytes 49156
  305.7 17.7 %copy-start.36 = (f32[8]{0:T(128)S(1)}, f32[8]{0:T(128)}, u32[]{:S(2)}) copy-start(f32[8]{0:T(128)} %copy-done.35) | copy-start | bytes 100
  305.7 17.7 %copy-start.43 = (f32[1,8]{1,0:T(1,128)S(1)}, f32[1,8]{1,0:T(1,128)}, u32[]{:S(2)}) copy-start(f32[1,8]{1,0:T(1,128)} %param.28) | copy-start | bytes 100
  313.0 17.1 %copy-start.33 = (f32[1,512]{1,0:T(1,128)S(1)}, f32[1,512]{1,0:T(1,128)}, u32[]{:S(2)}) copy-start(f32[1,512]{1,0:T(1,128)} %param.29) | copy-start | bytes 6148
  313.0 10.4 %collective-permute-start.6 = (f32[8,65,128]{2,1,0:T(8,128)S(1)}, f32[8,65,128]{2,1,0:T(8,128)S(1)}, u32[]{:S(2)}, u32[]{:S(2)}) collective-permute-start(f32[8,65,128]{2,1,0:T(8,128)S(1)} %pad_maximum_fusion.6), channel_id=1, source_target_pairs={{0,128},{8,136},{16,144},{24,152},{32,160},{40,168},{48,176},{56,1... | collective-permute-start | bytes 798728 | tf_op jit(solution)/shard_map/ppermute | solution.py:15
  (12 other events, 37.2 us)
Sparse Core Ops, SparseCore 0:
  9.8 16.6 all-gather.1
  41.6 101.4 reduce-scatter.1
where the time goes:
time: 340 us; the launch traced here: 338 us
  waiting for transfers between devices  164 us (48%)
  other arithmetic  51.4 us (15%)
  starting transfers between devices  42.1 us (12%)
  matrix products  31.3 us (9%)
  between operations  22.6 us (7%)
  local copies, waits for them, and re-layouts  22 us (6%)
  blocking collectives  4.56 us (1%)
    reduce_scatter x1, waiting for transfers between devices, shards(): lax.psum_scatter(jnp.concatenate(pieces, axis=2), 'col', scatter_dimensio...  74.4 us
    ppermute x12, waiting for transfers between devices, from_behind(): lax.ppermute(value, axis, [(source, source + steps) for source in range(f...  70.8 us
    ppermute x12, starting transfers between devices, from_behind(): lax.ppermute(value, axis, [(source, source + steps) for source in range(f...  42 us
    all_gather x1, waiting for transfers between devices, shards(): tokens = lax.all_gather(hidden, 'row', axis=0, tiled=True)  18.5 us
    dot_general x4, matrix products, shards(): jnp.einsum('td,dgc->gtc', tokens, weight, preferred_element_type=jnp.floa...  10.4 us
    dot_general x6, matrix products, convolve(): from_edge = jnp.dot(picker, table, preferred_element_type=jnp.float32)  7.59 us
    slice x9, local copies, waits for them, and re-layouts, unpack(): return (packed[:, p_n, 0], packed[:, :p_n], packed[0, p_n, n_n - 1])  7.41 us
    dot_general x1, matrix products, local_terms(): jnp.einsum('hij,jhp->ihp', mixing, x_vals.astype(jnp.float32), precision=...  6.86 us
  transfers between devices with their start and end apart: 14, of which 9 were waited for; matrix products, arithmetic and copies ran while one was open for 18% of the time, Pallas kernels for 0%

commit v1 on v0

--- a/solution.py
+++ b/solution.py
@@ -7,6 +7,16 @@
 N = 128
 PRECISE = lax.Precision.HIGHEST
 EPSILON = 1e-05
+
+
+def _pass_terms(frame_in, a_name="row"):
+    shaped = jnp.concatenate(
+        lax.all_to_all(
+            jnp.stack([frame_in] * lax.axis_size(a_name)), a_name, split_axis=0, concat_axis=0
+        ),
+        axis=0,
+    )
+    return shaped
 
 
 def from_behind(value, axis, steps):
@@ -115,7 +125,7 @@
     conv_x_edges,
     conv_bc_edges,
 ):
-    tokens = lax.all_gather(hidden, "row", axis=0, tiled=True)
+    tokens = _pass_terms(hidden)
     rows_here = tokens.shape[0]
     channels = w_x.shape[2]
     heads_here = w_dt.shape[2]

time: 340 us -> 318 us (0.935)
  waiting for transfers between devices: 164 us -> 156 us
  other arithmetic: 51.4 us -> 44.9 us
  starting transfers between devices: 42.1 us -> 35.7 us
  blocking collectives: 4.56 us -> 9.6 us
  matrix products: 31.3 us -> 26.3 us
    all_gather x1 -> x0, waiting for transfers between devices: 18.5 us -> none  [shards(): tokens = lax.all_gather(hidden, 'row', axis=0, tiled=True)]
    ppermute x12, waiting for transfers between devices: 70.8 us -> 79.5 us  [from_behind(): lax.ppermute(value, axis, [(source, source + steps) for source in range(f...]
    ppermute x12, starting transfers between devices: 42 us -> 35.7 us  [from_behind(): lax.ppermute(value, axis, [(source, source + steps) for source in range(f...]
    all_to_all x0 -> x1, blocking collectives: none -> 4.88 us  [_pass_terms(): lax.all_to_all(jnp.stack([frame_in] * lax.axis_size(a_name)), a_name, spl...]
    dot_general x4 -> x3, matrix products: 10.4 us -> 6.49 us  [shards(): jnp.einsum('td,dgc->gtc', tokens, weight, preferred_element_type=jnp.floa...]
  transfers between devices with their start and end apart: 14 -> 13, of which waited for: 9 -> 9; matrix products, arithmetic and copies ran while one was open for 18% -> 15% of each run, Pallas kernels for 0% -> 0%
where the time goes in v1:
time: 318 us; the launch traced here: 315 us
  waiting for transfers between devices  156 us (49%)
  other arithmetic  44.9 us (14%)
  starting transfers between devices  35.7 us (11%)
  matrix products  26.3 us (8%)
  between operations  23 us (7%)
  local copies, waits for them, and re-layouts  19.2 us (6%)
  blocking collectives  9.6 us (3%)
    ppermute x12, waiting for transfers between devices, from_behind(): lax.ppermute(value, axis, [(source, source + steps) for source in range(f...  79.5 us
    reduce_scatter x1, waiting for transfers between devices, shards(): lax.psum_scatter(jnp.concatenate(pieces, axis=2), 'col', scatter_dimensio...  76.6 us
    ppermute x12, starting transfers between devices, from_behind(): lax.ppermute(value, axis, [(source, source + steps) for source in range(f...  35.7 us
    dot_general x6, matrix products, convolve(): from_edge = jnp.dot(picker, table, preferred_element_type=jnp.float32)  7.71 us
    dot_general x1, matrix products, local_terms(): jnp.einsum('hij,jhp->ihp', mixing, x_vals.astype(jnp.float32), precision=...  7.06 us
    dot_general x3, matrix products, shards(): jnp.einsum('td,dgc->gtc', tokens, weight, preferred_element_type=jnp.floa...  6.49 us
  transfers between devices with their start and end apart: 13, of which 9 were waited for; matrix products, arithmetic and copies ran while one was open for 15% of the time, Pallas kernels for 0%

profile of v1, /device:TPU:101, one launch (start us, length us, event | category | flops | bytes accessed | tf_op | source)
XLA Modules:
  0.0 314.9 jit_solution(6403444459835059835)
XLA Ops:
  7.2 1.4 pad_maximum_fusion.1
  8.7 4.9 %all_to_all.5 = bf16[2,256,1024]{2,1,0:T(8,128)(2,1)S(1)} all-to-all(bf16[2,256,1024]{2,1,0:T(8,128)(2,1)S(1)} %pad_maximum_fusion.1), channel_id=1, replica_groups=mesh['seq'=32,'row'=2,'col'=4] {'row'}, dimensions={0} | all-to-all | bytes 2097152 | tf_op jit(solution)/shard_map/all_to_all | solution.py:14
  13.5 1.3 fusion.30
  15.7 2.6 fusion.23
  18.4 2.6 fusion.20
  21.4 4.4 %pad_maximum_fusion = f32[4,512,1288]{1,2,0:T(8,128)} fusion(f32[4,512,8]{1,2,0:T(8,128)S(1)} %convolution_bitcast_fusion, f32[4,512,256]{1,2,0:T(8,128)S(1)} %fusion.30, f32[4,512,512]{1,2,0:T(8,128)S(1)} %fusion.23, f32[4,512,512]{1,2,0:T(8,128)S(1)} %fusion.20), kind=kLoop, calls=%fused_computation.5 | loop fusion | flops 7913472 | bytes 21102592 | tf_op jit(solution)/shard_map/concatenate | solution.py:138
  37.9 1.2 broadcast_compare_fusion.5
  39.1 1.2 iota_compare_fusion.16
  40.3 1.2 broadcast_compare_fusion.3
  48.5 1.1 fusion.69
  50.1 1.4 fusion.70
  51.5 76.6 %reduce-scatter.2.cloned.1.call-done = f32[1,512,1288]{1,2,0:T(8,128)} async-done(((f32[4,512,1288]{1,2,0:T(8,128)}), f32[1,512,1288]{1,2,0:T(8,128)}) %reduce-scatter.2.cloned.1.call-update) | async-done | bytes 2637840 | tf_op jit(solution)/shard_map/reduce_scatter | solution.py:137
  128.1 1.9 convert_bitcast_fusion
  130.2 4.5 %collective-permute-start = (bf16[3,512]{0,1:T(8,128)(2,1)S(1)}, bf16[3,512]{0,1:T(8,128)(2,1)}, u32[]{:S(2)}, u32[]{:S(2)}) collective-permute-start(bf16[3,512]{0,1:T(8,128)(2,1)S(1)} %slice_select_fusion), channel_id=1, source_target_pairs={{0,8},{8,16},{16,24},{24,32},{32,40},{40,48},{48,56},{56,64},{64,7... | collective-permute-start | bytes 9224 | tf_op jit(solution)/shard_map/ppermute | solution.py:25
  135.5 2.5 collective-permute-start.1
  138.7 1.1 reduce-window.60
  143.2 1.8 multiply_convert_fusion.2
  145.0 2.6 multiply_convert_fusion.1
  147.8 2.1 fusion.11
  151.5 2.9 collective-permute-start.7
  155.5 6.6 %collective-permute-done.7 = f32[8,65,128]{2,1,0:T(8,128)} collective-permute-done((f32[8,65,128]{2,1,0:T(8,128)}, f32[8,65,128]{2,1,0:T(8,128)}, u32[]{:S(2)}, u32[]{:S(2)}) %collective-permute-start.7) | collective-permute-done | bytes 266272 | tf_op jit(solution)/shard_map/ppermute | solution.py:25
  163.1 1.3 slice.309
  167.0 1.9 collective-permute-start.8
  170.3 14.6 %collective-permute-done.8 = f32[8,65,128]{2,1,0:T(8,128)S(1)} collective-permute-done((f32[8,65,128]{2,1,0:T(8,128)}, f32[8,65,128]{2,1,0:T(8,128)S(1)}, u32[]{:S(2)}, u32[]{:S(2)}) %collective-permute-start.8) | collective-permute-done | bytes 266272 | tf_op jit(solution)/shard_map/ppermute | solution.py:25
  187.3 4.2 %collective-permute-start.9 = (f32[8,65,128]{2,1,0:T(8,128)}, f32[8,65,128]{2,1,0:T(8,128)}, u32[]{:S(2)}, u32[]{:S(2)}) collective-permute-start(f32[8,65,128]{2,1,0:T(8,128)} %pad_maximum_fusion.10), channel_id=1, source_target_pairs={{32,0},{40,8},{48,16},{56,24},{64,32},{72,40},{80,48},{88,56},{96,... | collective-permute-start | bytes 798728 | tf_op jit(solution)/shard_map/ppermute | solution.py:25
  191.5 1.3 slice_add_fusion
  192.9 15.3 %collective-permute-done.9 = f32[8,65,128]{2,1,0:T(8,128)} collective-permute-done((f32[8,65,128]{2,1,0:T(8,128)}, f32[8,65,128]{2,1,0:T(8,128)}, u32[]{:S(2)}, u32[]{:S(2)}) %collective-permute-start.9) | collective-permute-done | bytes 266272 | tf_op jit(solution)/shard_map/ppermute | solution.py:25
  209.1 1.3 slice.315
  212.9 1.9 collective-permute-start.10
  214.8 1.1 fusion.45
  216.7 1.9 collective-permute-start.2
  218.6 4.0 %collective-permute-done.10 = f32[8,65,128]{2,1,0:T(8,128)S(1)} collective-permute-done((f32[8,65,128]{2,1,0:T(8,128)}, f32[8,65,128]{2,1,0:T(8,128)S(1)}, u32[]{:S(2)}, u32[]{:S(2)}) %collective-permute-start.10) | collective-permute-done | bytes 266272 | tf_op jit(solution)/shard_map/ppermute | solution.py:25
  225.1 2.0 collective-permute-start.11
  230.1 1.5 collective-permute-done.11
  232.5 1.4 fusion.56
  233.9 1.9 collective-permute-start.3
  235.9 1.4 fusion.47
  237.3 14.7 %collective-permute-done.3 = f32[8,65,128]{2,1,0:T(8,128)S(1)} collective-permute-done((f32[8,65,128]{2,1,0:T(8,128)S(1)}, f32[8,65,128]{2,1,0:T(8,128)S(1)}, u32[]{:S(2)}, u32[]{:S(2)}) %collective-permute-start.3) | collective-permute-done | bytes 266272 | tf_op jit(solution)/shard_map/ppermute | solution.py:25
  252.4 3.0 collective-permute-start.4
  256.2 14.9 %collective-permute-done.4 = f32[8,65,128]{2,1,0:T(8,128)S(1)} collective-permute-done((f32[8,65,128]{2,1,0:T(8,128)S(1)}, f32[8,65,128]{2,1,0:T(8,128)S(1)}, u32[]{:S(2)}, u32[]{:S(2)}) %collective-permute-start.4) | collective-permute-done | bytes 266272 | tf_op jit(solution)/shard_map/ppermute | solution.py:25
  271.5 7.6 %collective-permute-start.5 = (f32[8,65,128]{2,1,0:T(8,128)S(1)}, f32[8,65,128]{2,1,0:T(8,128)S(1)}, u32[]{:S(2)}, u32[]{:S(2)}) collective-permute-start(f32[8,65,128]{2,1,0:T(8,128)S(1)} %pad_maximum_fusion.6), channel_id=1, source_target_pairs={{0,64},{8,72},{16,80},{24,88},{32,96},{40,104},{48,112},{56,120},{... | collective-permute-start | bytes 798728 | tf_op jit(solution)/shard_map/ppermute | solution.py:25
  279.1 7.1 %fusion.38 = f32[512,8,64]{0,2,1:T(8,128)S(1)} fusion(bf16[512,8,64]{0,2,1:T(8,128)(2,1)S(1)} %bitcast.157, f32[8,512]{1,0:T(8,128)S(1)} %copy-done.18, f32[512,512]{1,0:T(8,128)S(1)} %fusion.89, f32[8,512]{1,0:T(8,128)S(1)} %add_bitcast_fusion.1, pred[512,512]{1,0:T(8,128)(4,1)S(1)} %copy-done.10, f32[512,8,64]{0,2,1:T(8,128)S(1)} %bitcast.159, ...), kind=kOutput, calls=%fused_computation.38 | convolution fusion | flops 1621622784 | bytes 3981312 | tf_op jit(solution)/shard_map/hij,jhp->ihp/dot_general | solution.py:46
  286.6 1.3 collective-permute-start.6
  289.0 7.9 %collective-permute-done.6 = f32[8,65,128]{2,1,0:T(8,128)S(1)} collective-permute-done((f32[8,65,128]{2,1,0:T(8,128)S(1)}, f32[8,65,128]{2,1,0:T(8,128)S(1)}, u32[]{:S(2)}, u32[]{:S(2)}) %collective-permute-start.6) | collective-permute-done | bytes 266272 | tf_op jit(solution)/shard_map/ppermute | solution.py:25
  297.6 1.4 multiply_reduce_fusion
  299.0 4.7 %psum.7 = f32[512]{0:T(512)S(1)} all-reduce(f32[512]{0:T(512)S(1)} %multiply_reduce_fusion), channel_id=1, replica_groups=mesh['seq'=32,'row'=2,'col'=4] {'row'}, use_global_device_ids=true, to_apply=%region_15.16 | all-reduce | flops 512 | bytes 4096 | tf_op jit(solution)/shard_map/psum | solution.py:249
  303.8 2.2 fusion.52
  306.0 2.0 copy.69
  (241 shorter events, 41.8 us)
Async XLA Ops:
  7.2 120.9 %reduce-scatter.2.cloned.1.call-start = ((), (), s32[]{:S(2)}) async-start(), calls=%async_computation.2 | async-start | bytes 13189120 | tf_op jit(solution)/shard_map/reduce_scatter | solution.py:137
  25.8 8.8 %copy-start.12 = (bf16[3,3,1,256]{3,1,2,0:T(4,128)(2,1)S(1)}, bf16[3,3,1,256]{3,1,2,0:T(4,128)(2,1)}, u32[]{:S(2)}) copy-start(bf16[3,3,1,256]{3,1,2,0:T(4,128)(2,1)} %param.33) | copy-start | bytes 13828
  25.8 9.6 %copy-start.37 = (bf16[1,256]{1,0:T(2,128)(2,1)S(1)}, bf16[1,256]{1,0:T(2,128)(2,1)}, u32[]{:S(2)}) copy-start(bf16[1,256]{1,0:T(2,128)(2,1)} %param.25) | copy-start | bytes 1540
  25.8 20.2 %copy-start.22 = (bf16[4,1,256]{2,0,1:T(4,128)(2,1)S(1)}, bf16[4,1,256]{2,0,1:T(4,128)(2,1)}, u32[]{:S(2)}) copy-start(bf16[4,1,256]{2,0,1:T(4,128)(2,1)} %param.23) | copy-start | bytes 6148
  25.8 20.8 %copy-start.19 = (bf16[4,1,512]{2,0,1:T(4,128)(2,1)S(1)}, bf16[4,1,512]{2,0,1:T(4,128)(2,1)}, u32[]{:S(2)}) copy-start(bf16[4,1,512]{2,0,1:T(4,128)(2,1)} %param.22) | copy-start | bytes 12292
  36.1 101.9 %copy-start.23 = (f32[1,8]{1,0:T(1,128)S(1)}, f32[1,8]{1,0:T(1,128)}, u32[]{:S(2)}) copy-start(f32[1,8]{1,0:T(1,128)} %param.26) | copy-start | bytes 100
  36.1 101.9 %copy-start.25 = (f32[1,8]{1,0:T(1,128)S(1)}, f32[1,8]{1,0:T(1,128)}, u32[]{:S(2)}) copy-start(f32[1,8]{1,0:T(1,128)} %param.27) | copy-start | bytes 100
  130.0 24.4 %copy-start.2 = (bf16[512,1288]{0,1:T(8,128)(2,1)}, bf16[512,1288]{0,1:T(8,128)(2,1)S(1)}, u32[]{:S(2)}) copy-start(bf16[512,1288]{0,1:T(8,128)(2,1)S(1)} %convert_bitcast_fusion) | copy-start | bytes 3956740
  130.0 14.9 %copy-start.30 = (f32[1,512]{1,0:T(1,128)S(1)}, f32[1,512]{1,0:T(1,128)}, u32[]{:S(2)}) copy-start(f32[1,512]{1,0:T(1,128)} %add.428) | copy-start | bytes 6148
  130.2 14.8 %copy-start.31 = (s32[512]{0:T(512)S(1)}, s32[512]{0:T(512)}, u32[]{:S(2)}) copy-start(s32[512]{0:T(512)} %get-tuple-element.29) | copy-start | bytes 6148
  130.2 14.8 %copy-start.32 = (f32[1,1,512]{2,0,1:T(1,128)S(1)}, f32[1,1,512]{2,0,1:T(1,128)}, u32[]{:S(2)}) copy-start(f32[1,1,512]{2,0,1:T(1,128)} %get-tuple-element.41) | copy-start | bytes 6148
  130.2 14.8 %copy-start.33 = (f32[1,1,512]{2,0,1:T(1,128)S(1)}, f32[1,1,512]{2,0,1:T(1,128)}, u32[]{:S(2)}) copy-start(f32[1,1,512]{2,0,1:T(1,128)} %get-tuple-element.42) | copy-start | bytes 6148
  130.2 14.8 %copy-start.34 = (f32[1,1,512]{2,0,1:T(1,128)S(1)}, f32[1,1,512]{2,0,1:T(1,128)}, u32[]{:S(2)}) copy-start(f32[1,1,512]{2,0,1:T(1,128)} %get-tuple-element.43) | copy-start | bytes 6148
  130.2 14.8 %copy-start.35 = (f32[1,1,512]{2,0,1:T(1,128)S(1)}, f32[1,1,512]{2,0,1:T(1,128)}, u32[]{:S(2)}) copy-start(f32[1,1,512]{2,0,1:T(1,128)} %get-tuple-element.44) | copy-start | bytes 6148
  130.2 14.8 %copy-start.41 = (pred[512]{0:T(512)(128)(4,1)S(1)}, pred[512]{0:T(512)(128)(4,1)}, u32[]{:S(2)}) copy-start(pred[512]{0:T(512)(128)(4,1)} %get-tuple-element.51) | copy-start | bytes 1540
  130.2 14.8 %copy-start.42 = (pred[512]{0:T(512)(128)(4,1)S(1)}, pred[512]{0:T(512)(128)(4,1)}, u32[]{:S(2)}) copy-start(pred[512]{0:T(512)(128)(4,1)} %get-tuple-element.52) | copy-start | bytes 1540
  130.2 14.8 %copy-start.43 = (pred[512]{0:T(512)(128)(4,1)S(1)}, pred[512]{0:T(512)(128)(4,1)}, u32[]{:S(2)}) copy-start(pred[512]{0:T(512)(128)(4,1)} %get-tuple-element.53) | copy-start | bytes 1540
  130.2 14.7 %collective-permute-start = (bf16[3,512]{0,1:T(8,128)(2,1)S(1)}, bf16[3,512]{0,1:T(8,128)(2,1)}, u32[]{:S(2)}, u32[]{:S(2)}) collective-permute-start(bf16[3,512]{0,1:T(8,128)(2,1)S(1)} %slice_select_fusion), channel_id=1, source_target_pairs={{0,8},{8,16},{16,24},{24,32},{32,40},{40,48},{48,56},{56,64},{64,7... | collective-permute-start | bytes 9224 | tf_op jit(solution)/shard_map/ppermute | solution.py:25
  135.5 7.7 %collective-permute-start.1 = (bf16[3,256]{0,1:T(8,128)(2,1)}, bf16[3,256]{0,1:T(8,128)(2,1)S(1)}, u32[]{:S(2)}, u32[]{:S(2)}) collective-permute-start(bf16[3,256]{0,1:T(8,128)(2,1)} %slice_select_fusion.1), channel_id=1, source_target_pairs={{0,8},{8,16},{16,24},{24,32},{32,40},{40,48},{48,56},{56,64},{64,7... | collective-permute-start | bytes 4616 | tf_op jit(solution)/shard_map/ppermute | solution.py:25
  147.7 22.4 %copy-start.4 = (bf16[512,512]{0,1:T(8,128)(2,1)}, bf16[512,512]{0,1:T(8,128)(2,1)S(1)}, u32[]{:S(2)}) copy-start(bf16[512,512]{0,1:T(8,128)(2,1)S(1)} %multiply_convert_fusion.1) | copy-start | bytes 1572868
  147.7 21.2 %copy-start.28 = (pred[3]{0:T(512)(128)(4,1)S(1)}, pred[3]{0:T(512)(128)(4,1)}, u32[]{:S(2)}) copy-start(pred[3]{0:T(512)(128)(4,1)} %broadcast_compare_fusion.5) | copy-start | bytes 13
  147.7 21.3 %copy-start.20 = (s32[1024]{0:T(1024)S(1)}, s32[1024]{0:T(1024)}, u32[]{:S(2)}) copy-start(s32[1024]{0:T(1024)} %pad_clamp_fusion.2) | copy-start | bytes 12292
  147.8 22.4 %copy-start.27 = (pred[512]{0:T(512)(128)(4,1)S(1)}, pred[512]{0:T(512)(128)(4,1)}, u32[]{:S(2)}) copy-start(pred[512]{0:T(512)(128)(4,1)} %broadcast_compare_fusion.1) | copy-start | bytes 1540
  151.5 10.7 %collective-permute-start.7 = (f32[8,65,128]{2,1,0:T(8,128)}, f32[8,65,128]{2,1,0:T(8,128)}, u32[]{:S(2)}, u32[]{:S(2)}) collective-permute-start(f32[8,65,128]{2,1,0:T(8,128)} %pad_maximum_fusion.8), channel_id=1, source_target_pairs={{8,0},{16,8},{24,16},{32,24},{40,32},{48,40},{56,48},{64,56},{72,6... | collective-permute-start | bytes 798728 | tf_op jit(solution)/shard_map/ppermute | solution.py:25
  166.2 48.6 %copy-start.40 = (pred[4]{0:T(512)(128)(4,1)S(1)}, pred[4]{0:T(512)(128)(4,1)}, u32[]{:S(2)}) copy-start(pred[4]{0:T(512)(128)(4,1)} %iota_compare_fusion.16) | copy-start | bytes 16
  167.0 17.9 %collective-permute-start.8 = (f32[8,65,128]{2,1,0:T(8,128)}, f32[8,65,128]{2,1,0:T(8,128)S(1)}, u32[]{:S(2)}, u32[]{:S(2)}) collective-permute-start(f32[8,65,128]{2,1,0:T(8,128)} %pad_maximum_fusion.9), channel_id=1, source_target_pairs={{16,0},{24,8},{32,16},{40,24},{48,32},{56,40},{64,48},{72,56},{80,... | collective-permute-start | bytes 798728 | tf_op jit(solution)/shard_map/ppermute | solution.py:25
  170.2 56.9 %copy-start.17 = (f32[8,4]{0,1:T(4,128)S(1)}, f32[8,4]{0,1:T(4,128)}, u32[]{:S(2)}) copy-start(f32[8,4]{0,1:T(4,128)} %copy-done.16) | copy-start | bytes 388
  187.3 20.9 %collective-permute-start.9 = (f32[8,65,128]{2,1,0:T(8,128)}, f32[8,65,128]{2,1,0:T(8,128)}, u32[]{:S(2)}, u32[]{:S(2)}) collective-permute-start(f32[8,65,128]{2,1,0:T(8,128)} %pad_maximum_fusion.10), channel_id=1, source_target_pairs={{32,0},{40,8},{48,16},{56,24},{64,32},{72,40},{80,48},{88,56},{96,... | collective-permute-start | bytes 798728 | tf_op jit(solution)/shard_map/ppermute | solution.py:25
  192.9 38.7 %copy-start.7 = (f32[8,65,128]{2,1,0:T(8,128)S(1)}, f32[8,65,128]{2,1,0:T(8,128)}, u32[]{:S(2)}) copy-start(f32[8,65,128]{2,1,0:T(8,128)} %copy-done.6) | copy-start | bytes 798724
  192.9 43.0 %copy-start.3 = (f32[3,1,8,64,128]{4,3,2,1,0:T(8,128)S(1)}, f32[3,1,8,64,128]{4,3,2,1,0:T(8,128)}, u32[]{:S(2)}) copy-start(f32[3,1,8,64,128]{4,3,2,1,0:T(8,128)} %param.31) | copy-start | bytes 2359300
  212.9 9.7 %collective-permute-start.10 = (f32[8,65,128]{2,1,0:T(8,128)}, f32[8,65,128]{2,1,0:T(8,128)S(1)}, u32[]{:S(2)}, u32[]{:S(2)}) collective-permute-start(f32[8,65,128]{2,1,0:T(8,128)} %pad_maximum_fusion.11), channel_id=1, source_target_pairs={{64,0},{72,8},{80,16},{88,24},{96,32},{104,40},{112,48},{120,56},{... | collective-permute-start | bytes 798728 | tf_op jit(solution)/shard_map/ppermute | solution.py:25
  216.7 11.2 %collective-permute-start.2 = (f32[8,65,128]{2,1,0:T(8,128)}, f32[8,65,128]{2,1,0:T(8,128)S(1)}, u32[]{:S(2)}, u32[]{:S(2)}) collective-permute-start(f32[8,65,128]{2,1,0:T(8,128)} %pad_maximum_fusion.3), channel_id=1, source_target_pairs={{0,8},{8,16},{16,24},{24,32},{32,40},{40,48},{48,56},{56,64},{64,7... | collective-permute-start | bytes 798728 | tf_op jit(solution)/shard_map/ppermute | solution.py:25
  225.1 6.5 %collective-permute-start.11 = (f32[8,65,128]{2,1,0:T(8,128)}, f32[8,65,128]{2,1,0:T(8,128)}, u32[]{:S(2)}, u32[]{:S(2)}) collective-permute-start(f32[8,65,128]{2,1,0:T(8,128)} %pad_maximum_fusion.12), channel_id=1, source_target_pairs={{128,0},{136,8},{144,16},{152,24},{160,32},{168,40},{176,48},{184,... | collective-permute-start | bytes 798728 | tf_op jit(solution)/shard_map/ppermute | solution.py:25
  227.9 24.5 %copy-start.8 = (f32[8,65,128]{2,1,0:T(8,128)}, f32[8,65,128]{2,1,0:T(8,128)S(1)}, u32[]{:S(2)}) copy-start(f32[8,65,128]{2,1,0:T(8,128)S(1)} %collective-permute-done.2) | copy-start | bytes 798724
  232.5 22.9 %copy-start.15 = (f32[512,3]{0,1:T(4,128)S(1)}, f32[512,3]{0,1:T(4,128)}, u32[]{:S(2)}) copy-start(f32[512,3]{0,1:T(4,128)} %copy.86) | copy-start | bytes 18436
  233.9 18.0 %collective-permute-start.3 = (f32[8,65,128]{2,1,0:T(8,128)S(1)}, f32[8,65,128]{2,1,0:T(8,128)S(1)}, u32[]{:S(2)}, u32[]{:S(2)}) collective-permute-start(f32[8,65,128]{2,1,0:T(8,128)S(1)} %pad_maximum_fusion.4), channel_id=1, source_target_pairs={{0,16},{8,24},{16,32},{24,40},{32,48},{40,56},{48,64},{56,72},{64,... | collective-permute-start | bytes 798728 | tf_op jit(solution)/shard_map/ppermute | solution.py:25
  237.2 41.8 %copy-start.5 = (bf16[512,512]{0,1:T(8,128)(2,1)S(1)}, bf16[512,512]{0,1:T(8,128)(2,1)}, u32[]{:S(2)}) copy-start(bf16[512,512]{0,1:T(8,128)(2,1)} %copy-done.4) | copy-start | bytes 1572868
  237.3 41.8 %copy-start.10 = (pred[512,512]{1,0:T(8,128)(4,1)S(1)}, pred[512,512]{1,0:T(8,128)(4,1)}, u32[]{:S(2)}) copy-start(pred[512,512]{1,0:T(8,128)(4,1)} %fusion.46) | copy-start | bytes 786436
  237.3 41.8 %copy-start.18 = (f32[8,512]{1,0:T(8,128)S(1)}, f32[8,512]{1,0:T(8,128)}, u32[]{:S(2)}) copy-start(f32[8,512]{1,0:T(8,128)} %get-tuple-element.34) | copy-start | bytes 49156
  252.4 18.8 %collective-permute-start.4 = (f32[8,65,128]{2,1,0:T(8,128)S(1)}, f32[8,65,128]{2,1,0:T(8,128)S(1)}, u32[]{:S(2)}, u32[]{:S(2)}) collective-permute-start(f32[8,65,128]{2,1,0:T(8,128)S(1)} %pad_maximum_fusion.5), channel_id=1, source_target_pairs={{0,32},{8,40},{16,48},{24,56},{32,64},{40,72},{48,80},{56,88},{64,... | collective-permute-start | bytes 798728 | tf_op jit(solution)/shard_map/ppermute | solution.py:25
  271.5 14.7 %collective-permute-start.5 = (f32[8,65,128]{2,1,0:T(8,128)S(1)}, f32[8,65,128]{2,1,0:T(8,128)S(1)}, u32[]{:S(2)}, u32[]{:S(2)}) collective-permute-start(f32[8,65,128]{2,1,0:T(8,128)S(1)} %pad_maximum_fusion.6), channel_id=1, source_target_pairs={{0,64},{8,72},{16,80},{24,88},{32,96},{40,104},{48,112},{56,120},{... | collective-permute-start | bytes 798728 | tf_op jit(solution)/shard_map/ppermute | solution.py:25
  279.1 8.8 %copy-start.38 = (pred[3]{0:T(512)(128)(4,1)S(1)}, pred[3]{0:T(512)(128)(4,1)}, u32[]{:S(2)}) copy-start(pred[3]{0:T(512)(128)(4,1)} %get-tuple-element.58) | copy-start | bytes 13
  279.1 17.7 %copy-start.9 = (f32[8,65,128]{2,1,0:T(8,128)S(1)}, f32[8,65,128]{2,1,0:T(8,128)}, u32[]{:S(2)}) copy-start(f32[8,65,128]{2,1,0:T(8,128)} %copy-done.8) | copy-start | bytes 798724
  279.1 17.7 %copy-start.13 = (f32[512,8]{0,1:T(8,128)S(1)}, f32[512,8]{0,1:T(8,128)}, u32[]{:S(2)}) copy-start(f32[512,8]{0,1:T(8,128)} %get-tuple-element.23) | copy-start | bytes 49156
  279.1 17.7 %copy-start.44 = (f32[1,8]{1,0:T(1,128)S(1)}, f32[1,8]{1,0:T(1,128)}, u32[]{:S(2)}) copy-start(f32[1,8]{1,0:T(1,128)} %param.28) | copy-start | bytes 100
  286.6 17.2 %copy-start.36 = (f32[1,512]{1,0:T(1,128)S(1)}, f32[1,512]{1,0:T(1,128)}, u32[]{:S(2)}) copy-start(f32[1,512]{1,0:T(1,128)} %param.29) | copy-start | bytes 6148
  286.6 10.2 %collective-permute-start.6 = (f32[8,65,128]{2,1,0:T(8,128)S(1)}, f32[8,65,128]{2,1,0:T(8,128)S(1)}, u32[]{:S(2)}, u32[]{:S(2)}) collective-permute-start(f32[8,65,128]{2,1,0:T(8,128)S(1)} %pad_maximum_fusion.7), channel_id=1, source_target_pairs={{0,128},{8,136},{16,144},{24,152},{32,160},{40,168},{48,176},{56,1... | collective-permute-start | bytes 798728 | tf_op jit(solution)/shard_map/ppermute | solution.py:25
  296.8 11.2 %copy-start.1 = (bf16[1024,4,256]{2,1,0:T(4,128)(2,1)S(1)}, bf16[1024,4,256]{2,1,0:T(4,128)(2,1)}, u32[]{:S(2)}) copy-start(bf16[1024,4,256]{2,1,0:T(4,128)(2,1)} %param.20) | copy-start | bytes 6291460
  (12 other events, 55.7 us)
Sparse Core Ops, SparseCore 0:
  26.0 102.1 reduce-scatter.1
